TPU v7x, 32 devices: a whole 2x2x4 slice. The times are simulated.
32 devices in a mesh: req: 8 (over z, y), tp: 4 (over x, core).
Axes of the slice: x: 2, y: 2, z: 4, core: 2. Of those that a mesh axis runs over, the one named last changes fastest.
Arguments:
- hidden: bfloat16 [4096, 2048], P('req', 'tp'), may hold values from -6 to 6
- queries: bfloat16 [4096, 2048], P('req', 'tp'), may hold values from -4 to 4
- new_keys: bfloat16 [4096, 512], P('req'), may hold values from -4 to 4
- new_values: bfloat16 [4096, 512], P('req'), may hold values from -6 to 6
- cache_keys: bfloat16 [384, 64, 512], P('req'), may hold values from -6 to 6
- cache_values: bfloat16 [384, 64, 512], P('req'), may hold values from -6 to 6
- out_weight: bfloat16 [2048, 2048], P('tp'), may hold values from -0.125 to 0.125
- attn_gain: bfloat16 [2048], P('tp'), may hold values from 0.099609375 to 1.8984375
- ple_input: bfloat16 [4096, 256], P('req'), may hold values from -6 to 6
- ple_gate_weight: bfloat16 [2048, 256], P('tp'), may hold values from -0.125 to 0.125
- ple_proj_weight: bfloat16 [256, 2048], P(None, 'tp'), may hold values from -0.375 to 0.375
- ple_gain: bfloat16 [2048], P('tp'), may hold values from 0.099609375 to 1.8984375
- page_holder: int32 [384, 1], P('req'), may hold values from 0 to 7; in each aligned block of 48 rows (0 to 47, 48 to 95, ...) at most 6 rows name the same one
- page_slot: int32 [384, 1], P('req'), may hold values from 0 to 47
- page_counts: int32 [8, 8], P('req'), may hold values from 1 to 12, 48 in all within a row
- last_fill: int32 [8, 8], P('req'), may hold values from 1 to 64
- row_counts: int32 [8, 8], P('req'), may hold values from 1 to 256, 512 in all within a row
Outputs:
- layer_out: bfloat16 [4096, 2048], P('req', 'tp')
Inputs may be any that keep to these rules, and one draw needn't show every extreme that they name: `page_holder`: within the 48 page references of one device's requests (aligned blocks), no req index is named more than 6 times; in some block one is named exactly 6 times. `page_counts`: the 8 counts of one device sum to 48; some count equals 12. `row_counts`: the 8 counts of one device sum to 512; some count equals 256.
All inputs are finite; a program needn't handle non-finite values.
Results may differ from a plain program's by a relative error of at most 0.0061.
Values may be sent and summed in bfloat16 or wider, within the bound.
No kernel may reach another device: no remote copies, remote signals or barrier semaphores. Data moves between devices by JAX's collectives and lax.ppermute only.
A program may use at most 128 MiB of HBM per device.

v0:
```python
import math
import jax
import jax.numpy as jnp
from jax import lax
from jax.sharding import PartitionSpec as P

D = 2048
HD = 256


def slot_lookup(positions, counts):
    starts = jnp.cumsum(counts) - counts
    owning = jnp.sum((positions[:, None] >= starts[None, :]).astype(jnp.int32), axis=1) - 1
    return (owning, starts)


def table_pick(table, owning):
    onehot = owning[:, None] == jnp.arange(table.shape[0], dtype=jnp.int32)[None, :]
    return jnp.sum(jnp.where(onehot, table[None, :], 0), axis=1)


def attend_masks(counts_of_pages, fill_row, counts_of_rows, page_len, page_total, row_total):
    key_index = jnp.arange(page_total * page_len, dtype=jnp.int32)
    page_ref = key_index // page_len
    within = key_index % page_len
    page_owner, page_starts = slot_lookup(page_ref, counts_of_pages)
    context_len = (counts_of_pages - 1) * page_len + fill_row
    position = (page_ref - table_pick(page_starts, page_owner)) * page_len + within
    valid = position < table_pick(context_len, page_owner)
    row_index = jnp.arange(row_total, dtype=jnp.int32)
    row_owner = slot_lookup(row_index, counts_of_rows)[0]
    context_mask = (row_owner[:, None] == page_owner[None, :]) & valid[None, :]
    causal = (row_owner[:, None] == row_owner[None, :]) & (row_index[None, :] <= row_index[:, None])
    return jnp.concatenate([context_mask, causal], axis=1)


def shards(
    hidden,
    queries,
    new_keys,
    new_values,
    cache_keys,
    cache_values,
    out_weight,
    attn_gain,
    ple_input,
    ple_gate_weight,
    ple_proj_weight,
    ple_gain,
    page_holder,
    page_slot,
    page_counts,
    last_fill,
    row_counts,
):
    row_total = hidden.shape[0]
    page_total = cache_keys.shape[0]
    page_len = cache_keys.shape[1]
    req_count = lax.axis_size("req")
    tp_index = lax.axis_index("tp")
    local_heads = queries.shape[1] // HD
    kv_head = tp_index // 2
    capacity = max(2, page_total // req_count)
    holders = page_holder[:, 0]
    places = page_slot[:, 0]
    ref_index = jnp.arange(page_total, dtype=jnp.int32)
    earlier = (holders[:, None] == holders[None, :]) & (ref_index[:, None] > ref_index[None, :])
    ranking = jnp.sum(earlier.astype(jnp.int32), axis=1)
    matched = (holders[:, None, None] == jnp.arange(req_count, dtype=jnp.int32)[None, :, None]) & (
        ranking[:, None, None] == jnp.arange(capacity, dtype=jnp.int32)[None, None, :]
    )
    request_table = jnp.sum(jnp.where(matched, places[:, None, None] + 1, 0), axis=0) - 1
    asked = lax.all_to_all(request_table, "req", split_axis=0, concat_axis=0, tiled=True)
    wanted = jnp.maximum(asked, 0)
    head_keys = lax.dynamic_slice_in_dim(cache_keys, kv_head * HD, HD, 2)
    head_values = lax.dynamic_slice_in_dim(cache_values, kv_head * HD, HD, 2)
    stacked = jnp.concatenate([head_keys, head_values], axis=2)
    arrival_index = holders * capacity + ranking
    outgoing = stacked[wanted]
    arrived = lax.all_to_all(outgoing, "req", split_axis=0, concat_axis=0, tiled=True)
    context = arrived.reshape(req_count * capacity, page_len, 2 * HD)[arrival_index]
    context_keys = context[:, :, :HD].reshape(page_total * page_len, HD)
    context_values = context[:, :, HD:].reshape(page_total * page_len, HD)
    fresh_keys = lax.dynamic_slice_in_dim(new_keys, kv_head * HD, HD, 1)
    fresh_values = lax.dynamic_slice_in_dim(new_values, kv_head * HD, HD, 1)
    all_keys = jnp.concatenate([context_keys, fresh_keys], axis=0)
    all_values = jnp.concatenate([context_values, fresh_values], axis=0)
    masking = attend_masks(
        page_counts[0], last_fill[0], row_counts[0], page_len, page_total, row_total
    )
    query_rows = queries.reshape(row_total, local_heads, HD)
    scores = jnp.einsum("rhd,kd->hrk", query_rows, all_keys, preferred_element_type=jnp.float32) * (
        1.0 / math.sqrt(HD)
    )
    scores = jnp.where(masking[None], scores, -1e30)
    highest = jnp.max(scores, axis=-1, keepdims=True)
    expo = jnp.exp(scores - highest)
    weights = (expo / jnp.sum(expo, axis=-1, keepdims=True)).astype(jnp.bfloat16)
    attention = jnp.einsum("hrk,kd->rhd", weights, all_values, preferred_element_type=jnp.float32)
    attention = attention.astype(jnp.bfloat16).reshape(row_total, local_heads * HD)
    partial_sum = jnp.dot(attention, out_weight, preferred_element_type=jnp.float32)
    columns = hidden.shape[1]
    summed = lax.psum(partial_sum, "tp")
    squares = jnp.sum(summed * summed, axis=1)
    local_part = lax.dynamic_slice_in_dim(summed, tp_index * columns, columns, 1)
    normed = (
        local_part
        * lax.rsqrt(squares / D + 1e-06)[:, None]
        * attn_gain.astype(jnp.float32)[None, :]
    )
    mixed_state = (hidden.astype(jnp.float32) + normed).astype(jnp.bfloat16)
    gate = lax.psum(jnp.dot(mixed_state, ple_gate_weight, preferred_element_type=jnp.float32), "tp")
    activated = (jax.nn.gelu(gate, approximate=True) * ple_input.astype(jnp.float32)).astype(
        jnp.bfloat16
    )
    lifted = jnp.dot(activated, ple_proj_weight, preferred_element_type=jnp.float32)
    lift_squares = lax.psum(jnp.sum(lifted * lifted, axis=1), "tp")
    lift_normed = (
        lifted
        * lax.rsqrt(lift_squares / D + 1e-06)[:, None]
        * ple_gain.astype(jnp.float32)[None, :]
    )
    return (mixed_state.astype(jnp.float32) + lift_normed).astype(jnp.bfloat16)


def solution(mesh):
    return jax.shard_map(
        shards,
        mesh=mesh,
        in_specs=(
            P("req", "tp"),
            P("req", "tp"),
            P("req", None),
            P("req", None),
            P("req", None, None),
            P("req", None, None),
            P("tp", None),
            P("tp"),
            P("req", None),
            P("tp", None),
            P(None, "tp"),
            P("tp"),
            P("req", None),
            P("req", None),
            P("req", None),
            P("req", None),
            P("req", None),
        ),
        out_specs=P("req", "tp"),
        check_vma=False,
    )
```

profile of v0, /device:TPU:0, one launch (start us, length us, event | category | flops | bytes accessed | tf_op | source)
XLA Modules:
  0.0 293.5 jit_solution(17418125813564555138)
XLA Ops:
  9.7 7.3 %all-to-all-start = ((s32[8,1,6]{2,1,0:T(1,128)}), s32[8,1,6]{2,1,0:T(1,128)S(1)}, u32[]{:S(2)}, u32[]{:S(2)}) async-start(s32[8,1,6]{2,1,0:T(1,128)} %copy.35), calls=%async_computation | async-start | bytes 8192 | tf_op jit(solution)/shard_map/all_to_all | solution.py:73
  17.0 2.2 constant_dynamic-slice_fusion.2
  19.3 2.0 pad_maximum_fusion
  21.2 2.2 all-to-all-done
  23.5 4.4 %gather_fusion = bf16[48,64,512]{2,1,0:T(8,128)(2,1)} fusion(bf16[48,64,512]{2,1,0:T(8,128)(2,1)} %pad_maximum_fusion, s32[1024]{0:T(1024)S(1)} %pad_clamp_fusion.1), kind=kCustom, calls=%fused_computation | custom fusion | bytes 6291648 | tf_op jit(solution)/shard_map/gather | solution.py:79
  28.0 4.6 %all-to-all-start.1 = ((bf16[8,6,64,512]{3,2,1,0:T(8,128)(2,1)}), bf16[8,6,64,512]{3,2,1,0:T(8,128)(2,1)}, u32[]{:S(2)}, u32[]{:S(2)}) async-start(bf16[8,6,64,512]{3,2,1,0:T(8,128)(2,1)} %bitcast.52), calls=%async_computation.1 | async-start | bytes 6291456 | tf_op jit(solution)/shard_map/all_to_all | solution.py:80
  34.8 2.4 compare_and_fusion
  37.1 1.7 pad_add_fusion
  38.8 63.4 %all-to-all-done.1 = bf16[8,6,64,512]{3,2,1,0:T(8,128)(2,1)} async-done(((bf16[8,6,64,512]{3,2,1,0:T(8,128)(2,1)}), bf16[8,6,64,512]{3,2,1,0:T(8,128)(2,1)}, u32[]{:S(2)}, u32[]{:S(2)}) %all-to-all-start.1) | async-done | bytes 3145760 | tf_op jit(solution)/shard_map/all_to_all | solution.py:80
  102.2 4.4 %gather_fusion.1 = bf16[48,64,512]{2,1,0:T(8,128)(2,1)} fusion(bf16[48,64,512]{2,1,0:T(8,128)(2,1)} %bitcast.4, s32[1024]{0:T(1024)S(1)} %pad_clamp_fusion), kind=kCustom, calls=%fused_computation.1 | custom fusion | bytes 6291648 | tf_op jit(solution)/shard_map/gather | solution.py:81
  106.7 4.0 %fusion.49 = (bf16[48,64,256]{2,1,0:T(8,128)(2,1)}, bf16[48,64,256]{2,1,0:T(8,128)(2,1)}) fusion(bf16[48,64,512]{2,1,0:T(8,128)(2,1)} %gather_fusion.1), kind=kLoop, calls=%fused_computation.97 | loop fusion | bytes 6291456 | tf_op jit(solution)/shard_map/slice | solution.py:83
  110.6 2.7 copy.37
  113.3 8.7 %fusion.8 = f32[3584,512,2]{1,0,2:T(8,128)} fusion(bf16[512,256]{1,0:T(8,128)(2,1)S(1)} %get-tuple-element.15, bf16[3072,256]{1,0:T(8,128)(2,1)} %bitcast.53, bf16[64,2,8,256]{3,2,1,0:T(8,128)(2,1)S(1)} %bitcast.55), kind=kOutput, calls=%fused_computation.19 | convolution fusion | flops 1882718208 | bytes 17039360 | tf_op jit(solution)/shard_map/rhd,kd->hrk/dot_general | solution.py:92
  122.0 17.1 %fusion.50 = (f32[2,512]{1,0:T(2,128)S(1)}, f32[2,512,3584]{1,2,0:T(8,128)}) fusion(f32[3584,512,2]{1,0,2:T(8,128)} %fusion.8, pred[512,3584]{0,1:T(8,128)(4,1)} %pad_add_fusion), kind=kOutput, calls=%fused_computation.98 | output fusion | flops 22023680 | bytes 31199232 | tf_op jit(solution)/shard_map/sub | solution.py:97
  139.1 7.7 %fusion.11 = bf16[256,2,512]{2,0,1:T(8,128)(2,1)S(1)} fusion(f32[2,512,3584]{1,2,0:T(8,128)} %get-tuple-element.12, f32[2,512]{1,0:T(2,128)S(1)} %get-tuple-element.11, bf16[512,256]{0,1:T(8,128)(2,1)S(1)} %copy.44, bf16[3072,256]{0,1:T(8,128)(2,1)} %copy.37), kind=kOutput, calls=%fused_computation.22 | convolution fusion | flops 1890320384 | bytes 17043456 | tf_op jit(solution)/shard_map/hrk,kd->rhd/dot_general | solution.py:99
  146.9 3.2 %fusion.51 = f32[512,2048]{1,0:T(8,128)} fusion(bf16[512,512]{0,1:T(8,128)(2,1)S(1)} %bitcast.56, bf16[512,2048]{1,0:T(8,128)(2,1)S(1)} %copy-done), kind=kOutput, calls=%fused_computation.99 | convolution fusion | flops 1073741824 | bytes 6815744 | tf_op jit(solution)/shard_map/dot_general | solution.py:101
  150.8 84.0 %all-reduce.3.cloned.1.call-done = f32[512,2048]{1,0:T(8,128)} async-done(((f32[512,2048]{1,0:T(8,128)}), f32[512,2048]{1,0:T(8,128)}) %all-reduce.3.cloned.1.call-update) | async-done | bytes 4194320 | tf_op jit(solution)/shard_map/psum | solution.py:103
  234.8 2.5 multiply_reduce_fusion
  237.4 1.5 add_convert_fusion.1
  240.0 33.5 %all-reduce.5.cloned.1.call-done = f32[512,256]{1,0:T(8,128)} async-done(((f32[512,256]{1,0:T(8,128)}), f32[512,256]{1,0:T(8,128)}) %all-reduce.5.cloned.1.call-update) | async-done | bytes 524304 | tf_op jit(solution)/shard_map/psum | solution.py:112
  273.4 2.7 multiply_reduce_fusion.1
  276.1 2.6 copy.40
  278.7 5.7 %psum.23 = f32[512]{0:T(512)S(1)} all-reduce(f32[512]{0:T(512)S(1)} %get-tuple-element.13), channel_id=1, replica_groups=mesh['req'=8,'tp'=4] {'tp'}, use_global_device_ids=true, to_apply=%region_14.15 | all-reduce | flops 512 | bytes 4096 | tf_op jit(solution)/shard_map/psum | solution.py:117
  284.4 2.2 add_convert_fusion
  (57 shorter events, 7.2 us)
Async XLA Ops:
  6.5 140.3 %copy-start = (bf16[512,2048]{1,0:T(8,128)(2,1)S(1)}, bf16[512,2048]{1,0:T(8,128)(2,1)}, u32[]{:S(2)}) copy-start(bf16[512,2048]{1,0:T(8,128)(2,1)} %param.23) | copy-start | bytes 6291460
  9.7 13.7 %all-to-all-start = ((s32[8,1,6]{2,1,0:T(1,128)}), s32[8,1,6]{2,1,0:T(1,128)S(1)}, u32[]{:S(2)}, u32[]{:S(2)}) async-start(s32[8,1,6]{2,1,0:T(1,128)} %copy.35), calls=%async_computation | async-start | bytes 8192 | tf_op jit(solution)/shard_map/all_to_all | solution.py:73
  28.0 4.7 %copy-start.8 = (s32[1,8]{1,0:T(1,128)S(1)}, s32[1,8]{1,0:T(1,128)}, u32[]{:S(2)}) copy-start(s32[1,8]{1,0:T(1,128)} %param.31) | copy-start | bytes 100
  28.0 4.9 %copy-start.10 = (s32[1,8]{1,0:T(1,128)S(1)}, s32[1,8]{1,0:T(1,128)}, u32[]{:S(2)}) copy-start(s32[1,8]{1,0:T(1,128)} %param.33) | copy-start | bytes 100
  28.0 5.0 %copy-start.4 = (bf16[512,512]{1,0:T(8,128)(2,1)S(1)}, bf16[512,512]{1,0:T(8,128)(2,1)}, u32[]{:S(2)}) copy-start(bf16[512,512]{1,0:T(8,128)(2,1)} %param.19) | copy-start | bytes 1572868
  28.0 6.2 %copy-start.9 = (s32[48,1]{0,1:T(1,128)S(1)}, s32[48,1]{0,1:T(1,128)}, u32[]{:S(2)}) copy-start(s32[48,1]{0,1:T(1,128)} %param.29) | copy-start | bytes 580
  28.0 6.3 %copy-start.7 = (s32[1,8]{1,0:T(1,128)S(1)}, s32[1,8]{1,0:T(1,128)}, u32[]{:S(2)}) copy-start(s32[1,8]{1,0:T(1,128)} %param.32) | copy-start | bytes 100
  28.0 74.2 %all-to-all-start.1 = ((bf16[8,6,64,512]{3,2,1,0:T(8,128)(2,1)}), bf16[8,6,64,512]{3,2,1,0:T(8,128)(2,1)}, u32[]{:S(2)}, u32[]{:S(2)}) async-start(bf16[8,6,64,512]{3,2,1,0:T(8,128)(2,1)} %bitcast.52), calls=%async_computation.1 | async-start | bytes 6291456 | tf_op jit(solution)/shard_map/all_to_all | solution.py:80
  32.6 202.2 %all-reduce.3.cloned.1.call-start = ((), (), s32[]{:S(2)}) async-start(), calls=%async_computation.2 | async-start | bytes 8388608 | tf_op jit(solution)/shard_map/psum | solution.py:103
  110.6 2.7 copy-start.1
  150.1 0.7 copy-start.5
  150.1 87.2 %copy-start.2 = (bf16[512,512]{1,0:T(8,128)(2,1)S(1)}, bf16[512,512]{1,0:T(8,128)(2,1)}, u32[]{:S(2)}) copy-start(bf16[512,512]{1,0:T(8,128)(2,1)} %param.17) | copy-start | bytes 1572868
  150.1 123.3 %all-reduce.5.cloned.1.call-start = ((), (), s32[]{:S(2)}) async-start(), calls=%async_computation.3 | async-start | bytes 1048576 | tf_op jit(solution)/shard_map/psum | solution.py:112
  150.8 88.0 %copy-start.3 = (bf16[512,256]{1,0:T(8,128)(2,1)S(1)}, bf16[512,256]{1,0:T(8,128)(2,1)}, u32[]{:S(2)}) copy-start(bf16[512,256]{1,0:T(8,128)(2,1)} %param.26) | copy-start | bytes 786436
  150.8 89.2 %copy-start.6 = (bf16[512]{0:T(512)(128)(2,1)S(1)}, bf16[512]{0:T(512)(128)(2,1)}, u32[]{:S(2)}) copy-start(bf16[512]{0:T(512)(128)(2,1)} %param.28) | copy-start | bytes 3076
Sparse Core Ops, SparseCore 0:
  150.3 84.5 all-reduce.2
  240.1 33.3 all-reduce.4
where the time goes:
time: 294 us
  waiting for transfers between devices  183 us (62%)
  other arithmetic  32.8 us (11%)
  matrix products  23.5 us (8%)
  local copies, waits for them, and re-layouts  22.9 us (8%)
  between operations  13.6 us (5%)
  starting transfers between devices  11.9 us (4%)
  blocking collectives  5.73 us (2%)
    psum x1, waiting for transfers between devices, shards(): summed = lax.psum(partial_sum, 'tp')  84 us
    all_to_all x1, waiting for transfers between devices, shards(): lax.all_to_all(outgoing, 'req', split_axis=0, concat_axis=0, tiled=True)  63.4 us
    psum x1, waiting for transfers between devices, shards(): lax.psum(jnp.dot(mixed_state, ple_gate_weight, preferred_element_type=jnp...  33.5 us
    sub x1, other arithmetic, shards(): expo = jnp.exp(scores - highest)  17.1 us
    dot_general x1, matrix products, shards(): jnp.einsum('rhd,kd->hrk', query_rows, all_keys, preferred_element_type=jn...  8.73 us
    dot_general x1, matrix products, shards(): jnp.einsum('hrk,kd->rhd', weights, all_values, preferred_element_type=jnp...  7.72 us
    all_to_all x1, starting transfers between devices, shards(): lax.all_to_all(request_table, 'req', split_axis=0, concat_axis=0, tiled=T...  7.28 us
  transfers between devices with their start and end apart: 4, of which 4 were waited for; matrix products, arithmetic and copies ran while one was open for 4% of the time, Pallas kernels for 0%

commit v1 on v0

--- a/solution.py
+++ b/solution.py
@@ -100,7 +100,7 @@
     attention = attention.astype(jnp.bfloat16).reshape(row_total, local_heads * HD)
     partial_sum = jnp.dot(attention, out_weight, preferred_element_type=jnp.float32)
     columns = hidden.shape[1]
-    summed = lax.psum(partial_sum, "tp")
+    summed = jnp.sum(lax.all_gather(partial_sum, "tp"), axis=0)
     squares = jnp.sum(summed * summed, axis=1)
     local_part = lax.dynamic_slice_in_dim(summed, tp_index * columns, columns, 1)
     normed = (

time: 294 us -> 325 us (1.11)
  waiting for transfers between devices: 183 us -> 202 us
  other arithmetic: 32.8 us -> 42.3 us
    all_gather x0 -> x1, waiting for transfers between devices: none -> 103 us  [shards(): summed = jnp.sum(lax.all_gather(partial_sum, 'tp'), axis=0)]
    psum x1 -> x0, waiting for transfers between devices: 84 us -> none  [shards(): summed = lax.psum(partial_sum, 'tp')]
    reduce_sum x0 -> x1, other arithmetic: none -> 10.1 us  [shards(): summed = jnp.sum(lax.all_gather(partial_sum, 'tp'), axis=0)]
  transfers between devices with their start and end apart: 4 -> 4, of which waited for: 4 -> 4; matrix products, arithmetic and copies ran while one was open for 4% -> 3% of each run, Pallas kernels for 0% -> 0%
where the time goes in v1:
time: 325 us; the launch traced here: 324 us
  waiting for transfers between devices  202 us (62%)
  other arithmetic  42.3 us (13%)
  local copies, waits for them, and re-layouts  25.1 us (8%)
  matrix products  23.4 us (7%)
  between operations  13.6 us (4%)
  starting transfers between devices  12.1 us (4%)
  blocking collectives  5.73 us (2%)
    all_gather x1, waiting for transfers between devices, shards(): summed = jnp.sum(lax.all_gather(partial_sum, 'tp'), axis=0)  103 us
    all_to_all x1, waiting for transfers between devices, shards(): lax.all_to_all(outgoing, 'req', split_axis=0, concat_axis=0, tiled=True)  63.4 us
    psum x1, waiting for transfers between devices, shards(): lax.psum(jnp.dot(mixed_state, ple_gate_weight, preferred_element_type=jnp...  33.3 us
    sub x1, other arithmetic, shards(): expo = jnp.exp(scores - highest)  17.1 us
    reduce_sum x1, other arithmetic, shards(): summed = jnp.sum(lax.all_gather(partial_sum, 'tp'), axis=0)  10.1 us
    dot_general x1, matrix products, shards(): jnp.einsum('rhd,kd->hrk', query_rows, all_keys, preferred_element_type=jn...  8.73 us
    dot_general x1, matrix products, shards(): jnp.einsum('hrk,kd->rhd', weights, all_values, preferred_element_type=jnp...  7.72 us
    all_to_all x1, starting transfers between devices, shards(): lax.all_to_all(request_table, 'req', split_axis=0, concat_axis=0, tiled=T...  7.28 us
  transfers between devices with their start and end apart: 4, of which 4 were waited for; matrix products, arithmetic and copies ran while one was open for 3% of the time, Pallas kernels for 0%

profile of v1, /device:TPU:0, one launch (start us, length us, event | category | flops | bytes accessed | tf_op | source)
XLA Modules:
  0.0 324.3 jit_solution(11310288367521696382)
XLA Ops:
  9.7 7.3 %all-to-all-start = ((s32[8,1,6]{2,1,0:T(1,128)}), s32[8,1,6]{2,1,0:T(1,128)S(1)}, u32[]{:S(2)}, u32[]{:S(2)}) async-start(s32[8,1,6]{2,1,0:T(1,128)} %copy.40), calls=%async_computation | async-start | bytes 8192 | tf_op jit(solution)/shard_map/all_to_all | solution.py:73
  17.0 2.2 constant_dynamic-slice_fusion.3
  19.3 2.0 pad_maximum_fusion
  21.2 2.2 all-to-all-done
  23.5 4.4 %gather_fusion = bf16[48,64,512]{2,1,0:T(8,128)(2,1)} fusion(bf16[48,64,512]{2,1,0:T(8,128)(2,1)} %pad_maximum_fusion, s32[1024]{0:T(1024)S(1)} %pad_clamp_fusion.1), kind=kCustom, calls=%fused_computation | custom fusion | bytes 6291648 | tf_op jit(solution)/shard_map/gather | solution.py:79
  28.0 4.6 %all-to-all-start.1 = ((bf16[8,6,64,512]{3,2,1,0:T(8,128)(2,1)}), bf16[8,6,64,512]{3,2,1,0:T(8,128)(2,1)}, u32[]{:S(2)}, u32[]{:S(2)}) async-start(bf16[8,6,64,512]{3,2,1,0:T(8,128)(2,1)} %bitcast.54), calls=%async_computation.1 | async-start | bytes 6291456 | tf_op jit(solution)/shard_map/all_to_all | solution.py:80
  34.8 2.4 compare_and_fusion
  37.1 1.7 pad_add_fusion
  38.8 63.4 %all-to-all-done.1 = bf16[8,6,64,512]{3,2,1,0:T(8,128)(2,1)} async-done(((bf16[8,6,64,512]{3,2,1,0:T(8,128)(2,1)}), bf16[8,6,64,512]{3,2,1,0:T(8,128)(2,1)}, u32[]{:S(2)}, u32[]{:S(2)}) %all-to-all-start.1) | async-done | bytes 3145760 | tf_op jit(solution)/shard_map/all_to_all | solution.py:80
  102.2 4.4 %gather_fusion.1 = bf16[48,64,512]{2,1,0:T(8,128)(2,1)} fusion(bf16[48,64,512]{2,1,0:T(8,128)(2,1)} %bitcast.4, s32[1024]{0:T(1024)S(1)} %pad_clamp_fusion), kind=kCustom, calls=%fused_computation.1 | custom fusion | bytes 6291648 | tf_op jit(solution)/shard_map/gather | solution.py:81
  106.7 4.0 %fusion.49 = (bf16[48,64,256]{2,1,0:T(8,128)(2,1)}, bf16[48,64,256]{2,1,0:T(8,128)(2,1)}) fusion(bf16[48,64,512]{2,1,0:T(8,128)(2,1)} %gather_fusion.1), kind=kLoop, calls=%fused_computation.98 | loop fusion | bytes 6291456 | tf_op jit(solution)/shard_map/slice | solution.py:83
  110.6 2.7 copy.42
  113.3 8.7 %fusion.8 = f32[3584,512,2]{1,0,2:T(8,128)} fusion(bf16[512,256]{1,0:T(8,128)(2,1)S(1)} %get-tuple-element.15, bf16[3072,256]{1,0:T(8,128)(2,1)} %bitcast.55, bf16[64,2,8,256]{3,2,1,0:T(8,128)(2,1)S(1)} %bitcast.57), kind=kOutput, calls=%fused_computation.19 | convolution fusion | flops 1882718208 | bytes 17039360 | tf_op jit(solution)/shard_map/rhd,kd->hrk/dot_general | solution.py:92
  122.0 17.1 %fusion.50 = (f32[2,512]{1,0:T(2,128)S(1)}, f32[2,512,3584]{1,2,0:T(8,128)}) fusion(f32[3584,512,2]{1,0,2:T(8,128)} %fusion.8, pred[512,3584]{0,1:T(8,128)(4,1)} %pad_add_fusion), kind=kOutput, calls=%fused_computation.99 | output fusion | flops 22023680 | bytes 31199232 | tf_op jit(solution)/shard_map/sub | solution.py:97
  139.1 7.7 %fusion.11 = bf16[256,2,512]{2,0,1:T(8,128)(2,1)S(1)} fusion(f32[2,512,3584]{1,2,0:T(8,128)} %get-tuple-element.12, f32[2,512]{1,0:T(2,128)S(1)} %get-tuple-element.11, bf16[512,256]{0,1:T(8,128)(2,1)S(1)} %copy.50, bf16[3072,256]{0,1:T(8,128)(2,1)} %copy.42), kind=kOutput, calls=%fused_computation.22 | convolution fusion | flops 1890320384 | bytes 17043456 | tf_op jit(solution)/shard_map/hrk,kd->rhd/dot_general | solution.py:99
  146.9 3.2 fusion.51
  152.1 103.1 %all-gather.3.cloned.1.call-done = f32[2048,2048]{1,0:T(8,128)} async-done(((f32[512,2048]{1,0:T(8,128)}), f32[2048,2048]{1,0:T(8,128)}) %all-gather.3.cloned.1.call-update) | async-done | bytes 16777232 | tf_op jit(solution)/shard_map/all_gather | solution.py:103
  255.2 10.1 %reduce_sum.100 = f32[512,2048]{1,0:T(8,128)} reduce(f32[4,512,2048]{2,1,0:T(8,128)} %bitcast.53, f32[]{:T(128)} %constant.91.clone.1), dimensions={0}, to_apply=%region_10.11 | reduce | flops 3145728 | bytes 20971524 | tf_op jit(solution)/shard_map/reduce_sum | solution.py:103
  265.3 2.5 multiply_reduce_fusion
  270.6 1.6 add_convert_fusion.1
  273.4 33.3 %all-reduce.2.cloned.1.call-done = f32[512,256]{1,0:T(8,128)} async-done(((f32[512,256]{1,0:T(8,128)}), f32[512,256]{1,0:T(8,128)}) %all-reduce.2.cloned.1.call-update) | async-done | bytes 524304 | tf_op jit(solution)/shard_map/psum | solution.py:112
  306.7 2.6 multiply_reduce_fusion.1
  309.3 5.7 %psum.15 = f32[512]{0:T(512)S(1)} all-reduce(f32[512]{0:T(512)S(1)} %get-tuple-element.13), channel_id=1, replica_groups=mesh['req'=8,'tp'=4] {'tp'}, use_global_device_ids=true, to_apply=%region_14.15 | all-reduce | flops 512 | bytes 4096 | tf_op jit(solution)/shard_map/psum | solution.py:117
  315.0 1.4 add_convert_fusion
  (63 shorter events, 12.3 us)
Async XLA Ops:
  6.5 140.3 %copy-start = (bf16[512,2048]{1,0:T(8,128)(2,1)S(1)}, bf16[512,2048]{1,0:T(8,128)(2,1)}, u32[]{:S(2)}) copy-start(bf16[512,2048]{1,0:T(8,128)(2,1)} %param.23) | copy-start | bytes 6291460
  9.7 13.7 %all-to-all-start = ((s32[8,1,6]{2,1,0:T(1,128)}), s32[8,1,6]{2,1,0:T(1,128)S(1)}, u32[]{:S(2)}, u32[]{:S(2)}) async-start(s32[8,1,6]{2,1,0:T(1,128)} %copy.40), calls=%async_computation | async-start | bytes 8192 | tf_op jit(solution)/shard_map/all_to_all | solution.py:73
  28.0 4.7 %copy-start.8 = (s32[1,8]{1,0:T(1,128)S(1)}, s32[1,8]{1,0:T(1,128)}, u32[]{:S(2)}) copy-start(s32[1,8]{1,0:T(1,128)} %param.31) | copy-start | bytes 100
  28.0 4.9 %copy-start.11 = (s32[1,8]{1,0:T(1,128)S(1)}, s32[1,8]{1,0:T(1,128)}, u32[]{:S(2)}) copy-start(s32[1,8]{1,0:T(1,128)} %param.33) | copy-start | bytes 100
  28.0 5.0 %copy-start.4 = (bf16[512,512]{1,0:T(8,128)(2,1)S(1)}, bf16[512,512]{1,0:T(8,128)(2,1)}, u32[]{:S(2)}) copy-start(bf16[512,512]{1,0:T(8,128)(2,1)} %param.19) | copy-start | bytes 1572868
  28.0 6.2 %copy-start.10 = (s32[48,1]{0,1:T(1,128)S(1)}, s32[48,1]{0,1:T(1,128)}, u32[]{:S(2)}) copy-start(s32[48,1]{0,1:T(1,128)} %param.29) | copy-start | bytes 580
  28.0 6.3 %copy-start.7 = (s32[1,8]{1,0:T(1,128)S(1)}, s32[1,8]{1,0:T(1,128)}, u32[]{:S(2)}) copy-start(s32[1,8]{1,0:T(1,128)} %param.32) | copy-start | bytes 100
  28.0 74.2 %all-to-all-start.1 = ((bf16[8,6,64,512]{3,2,1,0:T(8,128)(2,1)}), bf16[8,6,64,512]{3,2,1,0:T(8,128)(2,1)}, u32[]{:S(2)}, u32[]{:S(2)}) async-start(bf16[8,6,64,512]{3,2,1,0:T(8,128)(2,1)} %bitcast.54), calls=%async_computation.1 | async-start | bytes 6291456 | tf_op jit(solution)/shard_map/all_to_all | solution.py:80
  32.6 222.6 %all-gather.3.cloned.1.call-start = ((), (), s32[]{:S(2)}) async-start(), calls=%async_computation.3 | async-start | bytes 20971520 | tf_op jit(solution)/shard_map/all_gather | solution.py:103
  110.6 2.7 copy-start.1
  150.1 1.0 copy-start.2
  150.1 2.0 copy-start.5
  150.1 156.6 %all-reduce.2.cloned.1.call-start = ((), (), s32[]{:S(2)}) async-start(), calls=%async_computation.2 | async-start | bytes 1048576 | tf_op jit(solution)/shard_map/psum | solution.py:112
  267.9 4.3 %copy-start.3 = (bf16[512,256]{1,0:T(8,128)(2,1)S(1)}, bf16[512,256]{1,0:T(8,128)(2,1)}, u32[]{:S(2)}) copy-start(bf16[512,256]{1,0:T(8,128)(2,1)} %param.26) | copy-start | bytes 786436
  269.2 4.1 %copy-start.6 = (bf16[512]{0:T(512)(128)(2,1)S(1)}, bf16[512]{0:T(512)(128)(2,1)}, u32[]{:S(2)}) copy-start(bf16[512]{0:T(512)(128)(2,1)} %param.28) | copy-start | bytes 3076
  270.5 36.1 %copy-start.9 = (bf16[256,512]{1,0:T(8,128)(2,1)S(1)}, bf16[256,512]{1,0:T(8,128)(2,1)}, u32[]{:S(2)}) copy-start(bf16[256,512]{1,0:T(8,128)(2,1)} %param.27) | copy-start | bytes 786436
Sparse Core Ops, SparseCore 0:
  150.2 104.9 all-gather.2
  273.5 33.1 all-reduce.1
